TPU v7x, 256 devices: a whole 4x4x8 slice. The times are simulated.
256 devices in a mesh: bz: 16 (over x_hi, y, core), bxy: 16 (over z, x_lo).
Axes of the slice: x: 4 (x_hi: 2, x_lo: 2; x = x_hi * 2 + x_lo), y: 4, z: 8, core: 2. Of those that a mesh axis runs over, the one named last changes fastest.
Arguments:
- estimate: float32 [128, 256, 512], P('bz', 'bxy'), may hold values from 0.5 to 2
- observed: bfloat16 [3, 128, 256, 512], P(None, 'bz', 'bxy'), may hold values from 0.5 to 2
- psf_taps: float32 [3, 3, 3, 9], replicated, may hold values from 0.05 to 1
- view_shift: int32 [3], replicated, may hold values from 0 to 511
- intersection: int32 [3, 16, 16], replicated, may hold values 0 or 1
Outputs:
- updated: float32 [128, 256, 512], P('bz', 'bxy')
All inputs are finite; a program needn't handle non-finite values.
Results may differ from a plain program's by a relative error of at most 0.0004.
Values may be sent and summed in bfloat16 or wider, within the bound.
No kernel may reach another device: no remote copies, remote signals or barrier semaphores. Data moves between devices by JAX's collectives and lax.ppermute only.
A program may use at most 64 MiB of HBM per device.

v0:
```python
import jax
import jax.numpy as jnp
from jax import lax
from jax.sharding import PartitionSpec as P

VIEWS = 3
RANK = 3
RADIUS = 4
PASSES = 8


EPS_TV = 0.25
TAU = 0.08
BACKGROUND = 0.1
HIGHEST = lax.Precision.HIGHEST
HIGH = lax.Precision.HIGH


def extended(cells, sides, width):
    for axis, dim in sides:
        count = lax.axis_size(axis)
        ends = count - 1
        head = lax.slice_in_dim(cells, 0, width, axis=dim)
        tail = lax.slice_in_dim(cells, cells.shape[dim] - width, cells.shape[dim], axis=dim)
        cells = jnp.concatenate(
            [
                lax.ppermute(tail, axis, [(i, (i + 1) % count) for i in range(ends)]),
                cells,
                lax.ppermute(head, axis, [((i + 1) % count, i) for i in range(ends)]),
            ],
            axis=dim,
        )
    return cells


def flux(diff):
    return diff / jnp.sqrt(diff * diff + EPS_TV)


def tv_pass(padded, z_lower, z_upper, x_lower, x_upper):
    field = padded[1:-1, 1:-1]
    cells_y = field.shape[2]
    along_j = lax.broadcasted_iota(jnp.int32, field.shape, 2)
    step_z = flux(padded[1:, 1:-1] - padded[:-1, 1:-1])
    step_x = flux(padded[1:-1, 1:] - padded[1:-1, :-1])
    step_y = flux(field[:, :, 1:] - field[:, :, :-1])
    pad_y = jnp.zeros(field.shape[:2] + (1,), field.dtype)
    up_y = jnp.concatenate([step_y, pad_y], axis=2)
    down_y = jnp.concatenate([pad_y, step_y], axis=2)
    total = jnp.zeros_like(field)
    total = total + -step_z[:-1] * z_lower[:, None, None]
    total = total + step_z[1:] * z_upper[:, None, None]
    total = total + -step_x[:, :-1] * x_lower[None, :, None]
    total = total + step_x[:, 1:] * x_upper[None, :, None]
    total = total + jnp.where(along_j >= 1, -down_y, 0.0)
    total = total + jnp.where(along_j < cells_y - 1, up_y, 0.0)
    return field + TAU * total


def band(taps, rows, cols):
    gap = lax.iota(jnp.int32, cols)[None, :] - lax.iota(jnp.int32, rows)[:, None]
    out = jnp.zeros(taps.shape[:-1] + (rows, cols), jnp.float32)
    for tap in range(taps.shape[-1]):
        out = out + jnp.where(gap == tap, taps[..., tap, None, None], 0.0)
    return out


def plane_matrices(kz, kx, cz, cx):
    wz = band(kz, cz, cz + 2 * RADIUS)
    wx = band(kx, cx, cx + 2 * RADIUS)
    wide = cx + 2 * RADIUS
    q = lax.iota(jnp.int32, cz * cx)
    p = lax.iota(jnp.int32, (cz + 2 * RADIUS) * wide)
    pick_qz = (q[:, None] // cx == lax.iota(jnp.int32, cz)[None, :]).astype(jnp.float32)
    pick_qx = (q[:, None] % cx == lax.iota(jnp.int32, cx)[None, :]).astype(jnp.float32)
    pick_pz = (lax.iota(jnp.int32, cz + 2 * RADIUS)[:, None] == p[None, :] // wide).astype(jnp.float32)
    pick_px = (lax.iota(jnp.int32, wide)[:, None] == p[None, :] % wide).astype(jnp.float32)
    full_z = jnp.einsum("qa,...ab,bp->...qp", pick_qz, wz, pick_pz, precision=HIGH)
    full_x = jnp.einsum("qa,...ab,bp->...qp", pick_qx, wx, pick_px, precision=HIGH)
    return full_z * full_x


def line_matrices(ky, shift, ny):
    rows = lax.iota(jnp.int32, ny)[None, :, None] + shift[:, None, None]
    rows = jnp.where(rows >= ny, rows - ny, rows)
    gap = rows - lax.iota(jnp.int32, ny)[None, None, :] + RADIUS
    gap = gap[:, None]
    out = jnp.zeros(ky.shape[:-1] + (ny, ny), jnp.float32)
    for tap in range(ky.shape[-1]):
        out = out + jnp.where(gap == tap, ky[..., tap, None, None], 0.0)
    return out


def local(estimate, observed, psf_taps, view_shift, intersection):
    cz_here, cx_here, cells_y = estimate.shape
    bricks_z = lax.axis_size("bz")
    bricks_x = lax.axis_size("bxy")
    cells_z = cz_here * bricks_z
    cells_x = cx_here * bricks_x
    brick_z = lax.axis_index("bz")
    brick_x = lax.axis_index("bxy")
    z_base = brick_z * cz_here
    x_base = brick_x * cx_here
    smoothed = extended(estimate, (("bz", 0),), PASSES)
    smoothed, view_shift = lax.optimization_barrier((smoothed, view_shift))
    smoothed = extended(smoothed, (("bxy", 1),), PASSES)
    zc = z_base - PASSES + lax.iota(jnp.int32, smoothed.shape[0])
    xc = x_base - PASSES + lax.iota(jnp.int32, smoothed.shape[1])
    masks = lax.optimization_barrier((
        ((zc >= 0) & (zc < cells_z)).astype(jnp.float32),
        ((xc >= 0) & (xc < cells_x)).astype(jnp.float32),
    ))
    z_in, x_in = masks
    for pass_index in range(PASSES):
        size_z = smoothed.shape[0] - 2
        size_x = smoothed.shape[1] - 2
        z0 = pass_index
        x0 = pass_index
        smoothed = tv_pass(
            smoothed,
            z_in[z0:z0 + size_z],
            z_in[z0 + 2:z0 + 2 + size_z],
            x_in[x0:x0 + size_x],
            x_in[x0 + 2:x0 + 2 + size_x],
        )
    sent = smoothed.astype(jnp.bfloat16)
    sent_pad = extended(sent, (("bz", 0), ("bxy", 1)), RADIUS)
    rows_pad = (cz_here + 2 * RADIUS) * (cx_here + 2 * RADIUS)
    rows = cz_here * cx_here
    sent_flat = sent_pad.astype(jnp.float32).reshape(rows_pad, cells_y)
    kernels = psf_taps / jnp.sum(psf_taps, axis=-1, keepdims=True)
    fwd_plane = plane_matrices(kernels[:, :, 0], kernels[:, :, 1], cz_here, cx_here)
    adj_plane = plane_matrices(kernels[:, :, 0, ::-1], kernels[:, :, 1, ::-1], cz_here, cx_here)
    lines = lax.optimization_barrier(line_matrices(kernels[:, :, 2], view_shift, cells_y))
    planes = jnp.einsum("vrqp,pj->vrqj", fwd_plane, sent_flat, precision=HIGH)
    images = jnp.einsum("vrqi,vrij->vqj", planes, lines, precision=HIGH) / RANK
    images = images.reshape(VIEWS, cz_here, cx_here, cells_y)
    flags = intersection[:, brick_z, brick_x]
    ratios = jnp.where(
        flags[:, None, None, None] > 0,
        observed.astype(jnp.float32) / (images + BACKGROUND),
        1.0,
    ).astype(jnp.bfloat16)
    ratio_pad = extended(ratios, (("bz", 1), ("bxy", 2)), RADIUS)
    ratio_flat = ratio_pad.astype(jnp.float32).reshape(VIEWS, rows_pad, cells_y)
    spread = jnp.einsum("vrqp,vpj->vrqj", adj_plane, ratio_flat, precision=HIGH)
    correction = jnp.einsum("vrqi,vrji->qj", spread, lines, precision=HIGH) / RANK
    correction = correction.reshape(cz_here, cx_here, cells_y)
    return smoothed * correction / VIEWS


def solution(mesh):
    return jax.shard_map(
        local,
        mesh=mesh,
        in_specs=(P("bz", "bxy", None), P(None, "bz", "bxy", None), P(), P(), P()),
        out_specs=P("bz", "bxy", None),
        check_vma=False,
    )
```

profile of v0, /device:TPU:132, one launch (start us, length us, event | category | flops | bytes accessed | tf_op | source)
XLA Modules:
  0.0 132.1 jit_solution(5448311855076102593)
XLA Ops:
  0.0 4.3 %collective-permute-start.1 = (f32[8,16,512]{2,1,0:T(8,128)}, f32[8,16,512]{2,1,0:T(8,128)S(1)}, u32[]{:S(2)}, u32[]{:S(2)}) collective-permute-start(f32[8,16,512]{2,1,0:T(8,128)} %param.5), channel_id=1, source_target_pairs={{16,0},{32,16},{48,32},{64,48},{80,64},{96,80},{112,96},{128,112},... | collective-permute-start | bytes 786440 | tf_op jit(solution)/shard_map/ppermute | solution.py:29
  4.3 1.9 %collective-permute-start = (f32[8,16,512]{2,1,0:T(8,128)}, f32[8,16,512]{2,1,0:T(8,128)S(1)}, u32[]{:S(2)}, u32[]{:S(2)}) collective-permute-start(f32[8,16,512]{2,1,0:T(8,128)} %param.5), channel_id=1, source_target_pairs={{0,16},{16,32},{32,48},{48,64},{64,80},{80,96},{96,112},{112,128},... | collective-permute-start | bytes 786440 | tf_op jit(solution)/shard_map/ppermute | solution.py:27
  6.8 0.7 fusion.306
  7.7 0.7 fusion.308
  8.4 0.7 fusion.307
  9.0 0.6 fusion.305
  9.9 0.8 reduce_sum.9
  10.7 0.8 broadcast_divide_fusion
  12.7 2.3 %fusion.285 = f32[384,3,3,128]{3,0,2,1:T(8,128)} fusion(f32[384,3,3,8]{0,3,2,1:T(8,128)S(1)} %fusion.143, s32[128]{0:T(128)S(1)} %and_select_fusion.1), kind=kOutput, calls=%fused_computation.424 | convolution fusion | flops 21234688 | bytes 1880576 | tf_op jit(solution)/shard_map/qa,...ab,bp->...qp/dot_general | solution.py:78
  15.4 1.1 fusion.266
  16.8 2.3 %fusion.287 = f32[384,3,3,128]{3,0,2,1:T(8,128)} fusion(f32[384,3,3,8]{0,3,2,1:T(8,128)S(1)} %fusion.172, s32[128]{0:T(128)S(1)} %and_select_fusion.1), kind=kOutput, calls=%fused_computation.425 | convolution fusion | flops 21234688 | bytes 1880576 | tf_op jit(solution)/shard_map/qa,...ab,bp->...qp/dot_general | solution.py:78
  19.2 0.8 fusion.300
  20.0 4.0 %collective-permute-start.2 = (f32[24,8,512]{2,1,0:T(8,128)}, f32[24,8,512]{2,1,0:T(8,128)S(1)}, u32[]{:S(2)}, u32[]{:S(2)}) collective-permute-start(f32[24,8,512]{2,1,0:T(8,128)} %get-tuple-element.54), channel_id=1, source_target_pairs={{0,1},{1,2},{2,3},{3,4},{4,5},{5,6},{6,7},{7,8},{8,9},{9,10},{10,1... | collective-permute-start | bytes 1179656 | tf_op jit(solution)/shard_map/ppermute | solution.py:27
  25.1 0.9 compare_reduce_fusion
  26.3 4.1 %collective-permute-start.3 = (f32[24,8,512]{2,1,0:T(8,128)S(1)}, f32[24,8,512]{2,1,0:T(8,128)S(1)}, u32[]{:S(2)}, u32[]{:S(2)}) collective-permute-start(f32[24,8,512]{2,1,0:T(8,128)S(1)} %get-tuple-element.53), channel_id=1, source_target_pairs={{1,0},{2,1},{3,2},{4,3},{5,4},{6,5},{7,6},{8,7},{9,8},{10,9},{11,1... | collective-permute-start | bytes 1179656 | tf_op jit(solution)/shard_map/ppermute | solution.py:29
  30.4 0.7 compare_select_fusion
  31.1 8.5 %collective-permute-done.2 = f32[24,8,512]{2,1,0:T(8,128)S(1)} collective-permute-done((f32[24,8,512]{2,1,0:T(8,128)}, f32[24,8,512]{2,1,0:T(8,128)S(1)}, u32[]{:S(2)}, u32[]{:S(2)}) %collective-permute-start.2) | collective-permute-done | bytes 393248 | tf_op jit(solution)/shard_map/ppermute | solution.py:27
  39.8 3.2 %collective-permute-done.3 = f32[24,8,512]{2,1,0:T(8,128)S(1)} collective-permute-done((f32[24,8,512]{2,1,0:T(8,128)S(1)}, f32[24,8,512]{2,1,0:T(8,128)S(1)}, u32[]{:S(2)}, u32[]{:S(2)}) %collective-permute-start.3) | collective-permute-done | bytes 393248 | tf_op jit(solution)/shard_map/ppermute | solution.py:29
  43.7 0.6 rsqrt_multiply_fusion.1
  44.4 1.6 %fusion.20 = f32[22,30,512]{2,1,0:T(8,128)S(1)} fusion(f32[22,31,512]{2,1,0:T(8,128)S(1)} %rsqrt_multiply_fusion.2, f32[23,30,512]{2,1,0:T(8,128)S(1)} %rsqrt_multiply_fusion, f32[24,32,512]{2,1,0:T(8,128)S(1)} %constant_dynamic-update-slice_fusion, f32[22,30,511]{2,1,0:T(8,128)S(1)} %rsqrt_multiply_fusion.1, f32[30]{0:T(128)S(1)} %get-tuple-element.113, ...), kind=kLoop, calls=%fused_computation.27 | loop fusion | flops 5406720 | bytes 9460560 | tf_op jit(solution)/shard_map/add | solution.py:57
  46.6 0.6 rsqrt_multiply_fusion.4
  47.2 1.5 %fusion.29 = f32[20,28,512]{2,1,0:T(8,128)S(1)} fusion(f32[20,29,512]{2,1,0:T(8,128)S(1)} %rsqrt_multiply_fusion.5, f32[21,28,512]{2,1,0:T(8,128)S(1)} %rsqrt_multiply_fusion.3, f32[22,30,512]{2,1,0:T(8,128)S(1)} %fusion.20, f32[20,28,511]{2,1,0:T(8,128)S(1)} %rsqrt_multiply_fusion.4, f32[28]{0:T(128)S(1)} %get-tuple-element.109, ...), kind=kLoop, calls=%fused_computation.46 | loop fusion | flops 4587520 | bytes 8027328 | tf_op jit(solution)/shard_map/add | solution.py:57
  49.3 0.5 rsqrt_multiply_fusion.7
  49.8 1.3 fusion.47
  51.9 0.8 fusion.57
  53.5 0.7 fusion.66
  54.8 0.8 fusion.75
  57.9 4.3 %collective-permute-start.5 = (bf16[4,16,512]{2,1,0:T(8,128)(2,1)S(1)}, bf16[4,16,512]{2,1,0:T(8,128)(2,1)S(1)}, u32[]{:S(2)}, u32[]{:S(2)}) collective-permute-start(bf16[4,16,512]{2,1,0:T(8,128)(2,1)S(1)} %get-tuple-element.60), channel_id=1, source_target_pairs={{16,0},{32,16},{48,32},{64,48},{80,64},{96,80},{112,96},{128,112},... | collective-permute-start | bytes 196616 | tf_op jit(solution)/shard_map/ppermute | solution.py:29
  62.1 1.9 %collective-permute-start.4 = (bf16[4,16,512]{2,1,0:T(8,128)(2,1)S(1)}, bf16[4,16,512]{2,1,0:T(8,128)(2,1)S(1)}, u32[]{:S(2)}, u32[]{:S(2)}) collective-permute-start(bf16[4,16,512]{2,1,0:T(8,128)(2,1)S(1)} %get-tuple-element.59), channel_id=1, source_target_pairs={{0,16},{16,32},{32,48},{48,64},{64,80},{80,96},{96,112},{112,128},... | collective-permute-start | bytes 196616 | tf_op jit(solution)/shard_map/ppermute | solution.py:27
  64.1 5.1 %fusion.10 = (pred[3,512,512]{2,1,0:T(8,128)(4,1)S(1)}, pred[3,512,512]{2,1,0:T(8,128)(4,1)S(1)}, pred[3,512,512]{2,1,0:T(8,128)(4,1)S(1)}, pred[3,512,512]{2,1,...) fusion(s32[3,512]{1,0:T(4,128)S(1)} %compare_select_fusion), kind=kLoop, calls=%fused_computation.12 | loop fusion | flops 8650752 | bytes 7084032 | tf_op jit(solution)/shard_map/eq | solution.py:90
  69.2 2.1 %collective-permute-done.4 = bf16[4,16,512]{2,1,0:T(8,128)(2,1)S(1)} collective-permute-done((bf16[4,16,512]{2,1,0:T(8,128)(2,1)S(1)}, bf16[4,16,512]{2,1,0:T(8,128)(2,1)S(1)}, u32[]{:S(2)}, u32[]{:S(2)}) %collective-permute-start.4) | collective-permute-done | bytes 65568 | tf_op jit(solution)/shard_map/ppermute | solution.py:27
  71.4 2.0 %collective-permute-start.7 = (bf16[16,4,512]{2,1,0:T(4,128)(2,1)S(1)}, bf16[16,4,512]{2,1,0:T(4,128)(2,1)S(1)}, u32[]{:S(2)}, u32[]{:S(2)}) collective-permute-start(bf16[16,4,512]{2,1,0:T(4,128)(2,1)S(1)} %get-tuple-element.58), channel_id=1, source_target_pairs={{1,0},{2,1},{3,2},{4,3},{5,4},{6,5},{7,6},{8,7},{9,8},{10,9},{11,1... | collective-permute-start | bytes 196616 | tf_op jit(solution)/shard_map/ppermute | solution.py:29
  73.4 3.9 %collective-permute-start.6 = (bf16[16,4,512]{2,1,0:T(4,128)(2,1)S(1)}, bf16[16,4,512]{2,1,0:T(4,128)(2,1)S(1)}, u32[]{:S(2)}, u32[]{:S(2)}) collective-permute-start(bf16[16,4,512]{2,1,0:T(4,128)(2,1)S(1)} %get-tuple-element.57), channel_id=1, source_target_pairs={{0,1},{1,2},{2,3},{3,4},{4,5},{5,6},{6,7},{7,8},{8,9},{9,10},{10,1... | collective-permute-start | bytes 196616 | tf_op jit(solution)/shard_map/ppermute | solution.py:27
  77.3 7.5 %select_add_fusion = f32[3,3,512,512]{3,2,0,1:T(8,128)S(1)} fusion(f32[3,3]{0,1:T(4,128)S(1)} %bitcast.90, f32[3,3]{0,1:T(4,128)S(1)} %bitcast.91, f32[3,3]{0,1:T(4,128)S(1)} %bitcast.92, f32[3,3]{0,1:T(4,128)S(1)} %bitcast.93, f32[3,3]{0,1:T(4,128)S(1)} %bitcast.94, f32[3,3]{0,1:T(4,128)S(1)} %bitcast.95, f32[3,3]{0,1:T(4,128)S(1)} %bitcast.96, ...), kind=kLoop, calls=%fused_computation.2 | loop fusion | flops 40108032 | bytes 16515396 | tf_op jit(solution)/shard_map/add | solution.py:90
  85.0 1.5 %fusion.11 = f32[3,3,128,512]{3,2,1,0:T(8,128)S(1)} fusion(bf16[384,512,1,1]{1,0,3,2:T(8,128)(2,1)S(1)} %bitcast.85, f32[384,3,3,128]{3,0,2,1:T(8,128)S(1)} %copy-done, f32[384,3,3,128]{3,0,2,1:T(8,128)S(1)} %fusion.266), kind=kOutput, calls=%fused_computation.13 | convolution fusion | flops 1359396864 | bytes 6291456 | tf_op jit(solution)/shard_map/vrqp,pj->vrqj/dot_general | solution.py:135
  86.5 3.6 %fusion.40 = f32[3,128,512]{2,1,0:T(8,128)S(1)} fusion(f32[3,3,128,512]{3,2,1,0:T(8,128)S(1)} %fusion.11, f32[3,3,512,512]{3,2,0,1:T(8,128)S(1)} %select_add_fusion), kind=kOutput, calls=%fused_computation.59 | convolution fusion | flops 1812332544 | bytes 12582912 | tf_op jit(solution)/shard_map/vrqi,vrij->vqj/dot_general | solution.py:136
  90.4 4.7 %collective-permute-start.9 = (bf16[3,4,16,512]{3,2,1,0:T(8,128)(2,1)S(1)}, bf16[3,4,16,512]{3,2,1,0:T(8,128)(2,1)S(1)}, u32[]{:S(2)}, u32[]{:S(2)}) collective-permute-start(bf16[3,4,16,512]{3,2,1,0:T(8,128)(2,1)S(1)} %get-tuple-element.56), channel_id=1, source_target_pairs={{16,0},{32,16},{48,32},{64,48},{80,64},{96,80},{112,96},{128,112},... | collective-permute-start | bytes 589832 | tf_op jit(solution)/shard_map/ppermute | solution.py:29
  95.2 1.9 %collective-permute-start.8 = (bf16[3,4,16,512]{3,2,1,0:T(8,128)(2,1)S(1)}, bf16[3,4,16,512]{3,2,1,0:T(8,128)(2,1)S(1)}, u32[]{:S(2)}, u32[]{:S(2)}) collective-permute-start(bf16[3,4,16,512]{3,2,1,0:T(8,128)(2,1)S(1)} %get-tuple-element.55), channel_id=1, source_target_pairs={{0,16},{16,32},{32,48},{48,64},{64,80},{80,96},{96,112},{112,128},... | collective-permute-start | bytes 589832 | tf_op jit(solution)/shard_map/ppermute | solution.py:27
  97.5 0.8 collective-permute-done.9
  98.3 10.1 %collective-permute-done.8 = bf16[3,4,16,512]{3,2,1,0:T(8,128)(2,1)S(1)} collective-permute-done((bf16[3,4,16,512]{3,2,1,0:T(8,128)(2,1)S(1)}, bf16[3,4,16,512]{3,2,1,0:T(8,128)(2,1)S(1)}, u32[]{:S(2)}, u32[]{:S(2)}) %collective-permute-start.8) | collective-permute-done | bytes 196640 | tf_op jit(solution)/shard_map/ppermute | solution.py:27
  108.6 5.7 %collective-permute-start.11 = (bf16[3,16,4,512]{3,2,1,0:T(4,128)(2,1)S(1)}, bf16[3,16,4,512]{3,2,1,0:T(4,128)(2,1)S(1)}, u32[]{:S(2)}, u32[]{:S(2)}) collective-permute-start(bf16[3,16,4,512]{3,2,1,0:T(4,128)(2,1)S(1)} %get-tuple-element.52), channel_id=1, source_target_pairs={{1,0},{2,1},{3,2},{4,3},{5,4},{6,5},{7,6},{8,7},{9,8},{10,9},{11,1... | collective-permute-start | bytes 589832 | tf_op jit(solution)/shard_map/ppermute | solution.py:29
  114.4 2.2 %collective-permute-start.10 = (bf16[3,16,4,512]{3,2,1,0:T(4,128)(2,1)S(1)}, bf16[3,16,4,512]{3,2,1,0:T(4,128)(2,1)S(1)}, u32[]{:S(2)}, u32[]{:S(2)}) collective-permute-start(bf16[3,16,4,512]{3,2,1,0:T(4,128)(2,1)S(1)} %get-tuple-element.51), channel_id=1, source_target_pairs={{0,1},{1,2},{2,3},{3,4},{4,5},{5,6},{6,7},{7,8},{8,9},{9,10},{10,1... | collective-permute-start | bytes 589832 | tf_op jit(solution)/shard_map/ppermute | solution.py:27
  116.6 1.1 multiply_bitcast_fusion
  117.7 6.3 %collective-permute-done.10 = bf16[3,16,4,512]{3,2,1,0:T(4,128)(2,1)S(1)} collective-permute-done((bf16[3,16,4,512]{3,2,1,0:T(4,128)(2,1)S(1)}, bf16[3,16,4,512]{3,2,1,0:T(4,128)(2,1)S(1)}, u32[]{:S(2)}, u32[]{:S(2)}) %collective-permute-start.10) | collective-permute-done | bytes 196640 | tf_op jit(solution)/shard_map/ppermute | solution.py:27
  124.0 0.8 pad_maximum_fusion
  124.9 1.5 %fusion.13 = f32[3,3,128,512]{3,2,0,1:T(8,128)S(1)} fusion(bf16[3,384,512,1]{2,1,0,3:T(8,128)(2,1)S(1)} %bitcast.83, f32[3,3,128,384]{2,3,1,0:T(8,128)S(1)} %multiply_bitcast_fusion), kind=kOutput, calls=%fused_computation.15 | convolution fusion | flops 1358954496 | bytes 5308416 | tf_op jit(solution)/shard_map/vrqp,vpj->vrqj/dot_general | solution.py:146
  126.3 5.0 %fusion.52 = f32[128,512]{1,0:T(8,128)S(1)} fusion(f32[3,3,128,512]{3,2,0,1:T(8,128)S(1)} %fusion.13, f32[3,3,512,512]{3,2,0,1:T(8,128)S(1)} %select_add_fusion), kind=kOutput, calls=%fused_computation.81 | convolution fusion | flops 1812004864 | bytes 12058624 | tf_op jit(solution)/shard_map/vrqi,vrji->qj/dot_general | solution.py:147
  131.4 0.7 multiply_multiply_fusion
  (152 shorter events, 11.3 us)
Async XLA Ops:
  0.0 19.2 %collective-permute-start.1 = (f32[8,16,512]{2,1,0:T(8,128)}, f32[8,16,512]{2,1,0:T(8,128)S(1)}, u32[]{:S(2)}, u32[]{:S(2)}) collective-permute-start(f32[8,16,512]{2,1,0:T(8,128)} %param.5), channel_id=1, source_target_pairs={{16,0},{32,16},{48,32},{64,48},{80,64},{96,80},{112,96},{128,112},... | collective-permute-start | bytes 786440 | tf_op jit(solution)/shard_map/ppermute | solution.py:29
  4.3 14.9 %collective-permute-start = (f32[8,16,512]{2,1,0:T(8,128)}, f32[8,16,512]{2,1,0:T(8,128)S(1)}, u32[]{:S(2)}, u32[]{:S(2)}) collective-permute-start(f32[8,16,512]{2,1,0:T(8,128)} %param.5), channel_id=1, source_target_pairs={{0,16},{16,32},{32,48},{48,64},{64,80},{80,96},{96,112},{112,128},... | collective-permute-start | bytes 786440 | tf_op jit(solution)/shard_map/ppermute | solution.py:27
  9.8 5.6 %copy-start.4 = (pred[16,24]{1,0:T(8,128)(4,1)}, pred[16,24]{1,0:T(8,128)(4,1)S(1)}, u32[]{:S(2)}) copy-start(pred[16,24]{1,0:T(8,128)(4,1)S(1)} %get-tuple-element.130) | copy-start | bytes 1156
  9.8 5.6 %copy-start.6 = (pred[16,24]{1,0:T(8,128)(4,1)}, pred[16,24]{1,0:T(8,128)(4,1)S(1)}, u32[]{:S(2)}) copy-start(pred[16,24]{1,0:T(8,128)(4,1)S(1)} %get-tuple-element.131) | copy-start | bytes 1156
  9.8 5.5 %copy-start.8 = (pred[16,24]{1,0:T(8,128)(4,1)}, pred[16,24]{1,0:T(8,128)(4,1)S(1)}, u32[]{:S(2)}) copy-start(pred[16,24]{1,0:T(8,128)(4,1)S(1)} %get-tuple-element.132) | copy-start | bytes 1156
  9.8 5.5 %copy-start.10 = (pred[16,24]{1,0:T(8,128)(4,1)}, pred[16,24]{1,0:T(8,128)(4,1)S(1)}, u32[]{:S(2)}) copy-start(pred[16,24]{1,0:T(8,128)(4,1)S(1)} %get-tuple-element.133) | copy-start | bytes 1156
  9.8 5.5 %copy-start.12 = (pred[16,24]{1,0:T(8,128)(4,1)}, pred[16,24]{1,0:T(8,128)(4,1)S(1)}, u32[]{:S(2)}) copy-start(pred[16,24]{1,0:T(8,128)(4,1)S(1)} %get-tuple-element.134) | copy-start | bytes 1156
  9.8 5.5 %copy-start.14 = (pred[16,24]{1,0:T(8,128)(4,1)}, pred[16,24]{1,0:T(8,128)(4,1)S(1)}, u32[]{:S(2)}) copy-start(pred[16,24]{1,0:T(8,128)(4,1)S(1)} %get-tuple-element.135) | copy-start | bytes 1156
  9.9 5.5 %copy-start.16 = (pred[16,24]{1,0:T(8,128)(4,1)}, pred[16,24]{1,0:T(8,128)(4,1)S(1)}, u32[]{:S(2)}) copy-start(pred[16,24]{1,0:T(8,128)(4,1)S(1)} %fusion.264) | copy-start | bytes 1156
  9.9 5.5 %copy-start.18 = (s32[384]{0:T(512)}, s32[384]{0:T(512)S(1)}, u32[]{:S(2)}) copy-start(s32[384]{0:T(512)S(1)} %fusion.280) | copy-start | bytes 4612
  9.9 5.5 %copy-start.28 = (s32[128]{0:T(128)}, s32[128]{0:T(128)S(1)}, u32[]{:S(2)}) copy-start(s32[128]{0:T(128)S(1)} %and_select_fusion) | copy-start | bytes 1540
  16.5 2.6 %copy-start.3 = (f32[8,16,512]{2,1,0:T(8,128)S(1)}, f32[8,16,512]{2,1,0:T(8,128)}, u32[]{:S(2)}) copy-start(f32[8,16,512]{2,1,0:T(8,128)} %param.5) | copy-start | bytes 786436
  20.0 19.7 %collective-permute-start.2 = (f32[24,8,512]{2,1,0:T(8,128)}, f32[24,8,512]{2,1,0:T(8,128)S(1)}, u32[]{:S(2)}, u32[]{:S(2)}) collective-permute-start(f32[24,8,512]{2,1,0:T(8,128)} %get-tuple-element.54), channel_id=1, source_target_pairs={{0,1},{1,2},{2,3},{3,4},{4,5},{5,6},{6,7},{7,8},{8,9},{9,10},{10,1... | collective-permute-start | bytes 1179656 | tf_op jit(solution)/shard_map/ppermute | solution.py:27
  26.3 16.7 %collective-permute-start.3 = (f32[24,8,512]{2,1,0:T(8,128)S(1)}, f32[24,8,512]{2,1,0:T(8,128)S(1)}, u32[]{:S(2)}, u32[]{:S(2)}) collective-permute-start(f32[24,8,512]{2,1,0:T(8,128)S(1)} %get-tuple-element.53), channel_id=1, source_target_pairs={{1,0},{2,1},{3,2},{4,3},{5,4},{6,5},{7,6},{8,7},{9,8},{10,9},{11,1... | collective-permute-start | bytes 1179656 | tf_op jit(solution)/shard_map/ppermute | solution.py:29
  55.7 0.6 copy-start.22
  55.7 0.7 copy-start.23
  55.7 0.7 copy-start.24
  55.7 0.7 copy-start.25
  56.9 0.6 copy-start.20
  56.9 0.6 copy-start.21
  56.9 0.7 copy-start.26
  56.9 0.7 copy-start.27
  57.9 11.3 %collective-permute-start.5 = (bf16[4,16,512]{2,1,0:T(8,128)(2,1)S(1)}, bf16[4,16,512]{2,1,0:T(8,128)(2,1)S(1)}, u32[]{:S(2)}, u32[]{:S(2)}) collective-permute-start(bf16[4,16,512]{2,1,0:T(8,128)(2,1)S(1)} %get-tuple-element.60), channel_id=1, source_target_pairs={{16,0},{32,16},{48,32},{64,48},{80,64},{96,80},{112,96},{128,112},... | collective-permute-start | bytes 196616 | tf_op jit(solution)/shard_map/ppermute | solution.py:29
  62.1 9.2 %collective-permute-start.4 = (bf16[4,16,512]{2,1,0:T(8,128)(2,1)S(1)}, bf16[4,16,512]{2,1,0:T(8,128)(2,1)S(1)}, u32[]{:S(2)}, u32[]{:S(2)}) collective-permute-start(bf16[4,16,512]{2,1,0:T(8,128)(2,1)S(1)} %get-tuple-element.59), channel_id=1, source_target_pairs={{0,16},{16,32},{32,48},{48,64},{64,80},{80,96},{96,112},{112,128},... | collective-permute-start | bytes 196616 | tf_op jit(solution)/shard_map/ppermute | solution.py:27
  71.4 13.4 %collective-permute-start.7 = (bf16[16,4,512]{2,1,0:T(4,128)(2,1)S(1)}, bf16[16,4,512]{2,1,0:T(4,128)(2,1)S(1)}, u32[]{:S(2)}, u32[]{:S(2)}) collective-permute-start(bf16[16,4,512]{2,1,0:T(4,128)(2,1)S(1)} %get-tuple-element.58), channel_id=1, source_target_pairs={{1,0},{2,1},{3,2},{4,3},{5,4},{6,5},{7,6},{8,7},{9,8},{10,9},{11,1... | collective-permute-start | bytes 196616 | tf_op jit(solution)/shard_map/ppermute | solution.py:29
  73.4 11.4 %collective-permute-start.6 = (bf16[16,4,512]{2,1,0:T(4,128)(2,1)S(1)}, bf16[16,4,512]{2,1,0:T(4,128)(2,1)S(1)}, u32[]{:S(2)}, u32[]{:S(2)}) collective-permute-start(bf16[16,4,512]{2,1,0:T(4,128)(2,1)S(1)} %get-tuple-element.57), channel_id=1, source_target_pairs={{0,1},{1,2},{2,3},{3,4},{4,5},{5,6},{6,7},{7,8},{8,9},{9,10},{10,1... | collective-permute-start | bytes 196616 | tf_op jit(solution)/shard_map/ppermute | solution.py:27
  77.3 7.7 %copy-start = (f32[384,3,3,128]{3,0,2,1:T(8,128)S(1)}, f32[384,3,3,128]{3,0,2,1:T(8,128)}, u32[]{:S(2)}) copy-start(f32[384,3,3,128]{3,0,2,1:T(8,128)} %fusion.285) | copy-start | bytes 5308420
  86.5 3.7 %copy-start.2 = (bf16[3,8,16,512]{3,2,1,0:T(8,128)(2,1)S(1)}, bf16[3,8,16,512]{3,2,1,0:T(8,128)(2,1)}, u32[]{:S(2)}) copy-start(bf16[3,8,16,512]{3,2,1,0:T(8,128)(2,1)} %param.6) | copy-start | bytes 1179652
  90.1 7.0 %copy-start.5 = (pred[16,24]{1,0:T(8,128)(4,1)S(1)}, pred[16,24]{1,0:T(8,128)(4,1)}, u32[]{:S(2)}) copy-start(pred[16,24]{1,0:T(8,128)(4,1)} %copy-done.4) | copy-start | bytes 1156
  90.1 7.0 %copy-start.7 = (pred[16,24]{1,0:T(8,128)(4,1)S(1)}, pred[16,24]{1,0:T(8,128)(4,1)}, u32[]{:S(2)}) copy-start(pred[16,24]{1,0:T(8,128)(4,1)} %copy-done.6) | copy-start | bytes 1156
  90.1 7.0 %copy-start.9 = (pred[16,24]{1,0:T(8,128)(4,1)S(1)}, pred[16,24]{1,0:T(8,128)(4,1)}, u32[]{:S(2)}) copy-start(pred[16,24]{1,0:T(8,128)(4,1)} %copy-done.8) | copy-start | bytes 1156
  90.1 7.0 %copy-start.11 = (pred[16,24]{1,0:T(8,128)(4,1)S(1)}, pred[16,24]{1,0:T(8,128)(4,1)}, u32[]{:S(2)}) copy-start(pred[16,24]{1,0:T(8,128)(4,1)} %copy-done.10) | copy-start | bytes 1156
  90.1 7.0 %copy-start.13 = (pred[16,24]{1,0:T(8,128)(4,1)S(1)}, pred[16,24]{1,0:T(8,128)(4,1)}, u32[]{:S(2)}) copy-start(pred[16,24]{1,0:T(8,128)(4,1)} %copy-done.12) | copy-start | bytes 1156
  90.1 7.0 %copy-start.15 = (pred[16,24]{1,0:T(8,128)(4,1)S(1)}, pred[16,24]{1,0:T(8,128)(4,1)}, u32[]{:S(2)}) copy-start(pred[16,24]{1,0:T(8,128)(4,1)} %copy-done.14) | copy-start | bytes 1156
  90.2 7.0 %copy-start.17 = (pred[16,24]{1,0:T(8,128)(4,1)S(1)}, pred[16,24]{1,0:T(8,128)(4,1)}, u32[]{:S(2)}) copy-start(pred[16,24]{1,0:T(8,128)(4,1)} %copy-done.16) | copy-start | bytes 1156
  90.2 7.0 %copy-start.19 = (s32[384]{0:T(512)S(1)}, s32[384]{0:T(512)}, u32[]{:S(2)}) copy-start(s32[384]{0:T(512)} %copy-done.18) | copy-start | bytes 4612
  90.4 26.2 %copy-start.1 = (f32[384,3,3,128]{3,0,2,1:T(8,128)S(1)}, f32[384,3,3,128]{3,0,2,1:T(8,128)}, u32[]{:S(2)}) copy-start(f32[384,3,3,128]{3,0,2,1:T(8,128)} %fusion.287) | copy-start | bytes 5308420
  90.4 26.2 %copy-start.29 = (s32[128]{0:T(128)S(1)}, s32[128]{0:T(128)}, u32[]{:S(2)}) copy-start(s32[128]{0:T(128)} %copy-done.28) | copy-start | bytes 1540
  90.4 7.9 %collective-permute-start.9 = (bf16[3,4,16,512]{3,2,1,0:T(8,128)(2,1)S(1)}, bf16[3,4,16,512]{3,2,1,0:T(8,128)(2,1)S(1)}, u32[]{:S(2)}, u32[]{:S(2)}) collective-permute-start(bf16[3,4,16,512]{3,2,1,0:T(8,128)(2,1)S(1)} %get-tuple-element.56), channel_id=1, source_target_pairs={{16,0},{32,16},{48,32},{64,48},{80,64},{96,80},{112,96},{128,112},... | collective-permute-start | bytes 589832 | tf_op jit(solution)/shard_map/ppermute | solution.py:29
  95.2 13.3 %collective-permute-start.8 = (bf16[3,4,16,512]{3,2,1,0:T(8,128)(2,1)S(1)}, bf16[3,4,16,512]{3,2,1,0:T(8,128)(2,1)S(1)}, u32[]{:S(2)}, u32[]{:S(2)}) collective-permute-start(bf16[3,4,16,512]{3,2,1,0:T(8,128)(2,1)S(1)} %get-tuple-element.55), channel_id=1, source_target_pairs={{0,16},{16,32},{32,48},{48,64},{64,80},{80,96},{96,112},{112,128},... | collective-permute-start | bytes 589832 | tf_op jit(solution)/shard_map/ppermute | solution.py:27
  108.6 9.1 %collective-permute-start.11 = (bf16[3,16,4,512]{3,2,1,0:T(4,128)(2,1)S(1)}, bf16[3,16,4,512]{3,2,1,0:T(4,128)(2,1)S(1)}, u32[]{:S(2)}, u32[]{:S(2)}) collective-permute-start(bf16[3,16,4,512]{3,2,1,0:T(4,128)(2,1)S(1)} %get-tuple-element.52), channel_id=1, source_target_pairs={{1,0},{2,1},{3,2},{4,3},{5,4},{6,5},{7,6},{8,7},{9,8},{10,9},{11,1... | collective-permute-start | bytes 589832 | tf_op jit(solution)/shard_map/ppermute | solution.py:29
  114.4 9.7 %collective-permute-start.10 = (bf16[3,16,4,512]{3,2,1,0:T(4,128)(2,1)S(1)}, bf16[3,16,4,512]{3,2,1,0:T(4,128)(2,1)S(1)}, u32[]{:S(2)}, u32[]{:S(2)}) collective-permute-start(bf16[3,16,4,512]{3,2,1,0:T(4,128)(2,1)S(1)} %get-tuple-element.51), channel_id=1, source_target_pairs={{0,1},{1,2},{2,3},{3,4},{4,5},{5,6},{6,7},{7,8},{8,9},{9,10},{10,1... | collective-permute-start | bytes 589832 | tf_op jit(solution)/shard_map/ppermute | solution.py:27
where the time goes:
time: 133 us; the launch traced here: 132 us
  starting transfers between devices  40.9 us (31%)
  other arithmetic  32.2 us (24%)
  waiting for transfers between devices  31.2 us (23%)
  matrix products  19.6 us (15%)
  local copies, waits for them, and re-layouts  7.1 us (5%)
    ppermute x6, waiting for transfers between devices, extended(): lax.ppermute(tail, axis, [(i, (i + 1) % count) for i in range(ends)])  27.1 us
    ppermute x6, starting transfers between devices, extended(): lax.ppermute(head, axis, [((i + 1) % count, i) for i in range(ends)])  25.1 us
    ppermute x6, starting transfers between devices, extended(): lax.ppermute(tail, axis, [(i, (i + 1) % count) for i in range(ends)])  15.8 us
    add x1, other arithmetic, line_matrices(): out = out + jnp.where(gap == tap, ky[..., tap, None, None], 0.0)  7.49 us
    add x7, other arithmetic, tv_pass(): return field + TAU * total  7.24 us
    div x24, other arithmetic, flux(): return diff / jnp.sqrt(diff * diff + EPS_TV)  6.49 us
    dot_general x4, matrix products, plane_matrices(): jnp.einsum('qa,...ab,bp->...qp', pick_qz, wz, pick_pz, precision=HIGH)  5.23 us
    eq x1, other arithmetic, line_matrices(): out = out + jnp.where(gap == tap, ky[..., tap, None, None], 0.0)  5.12 us
  transfers between devices with their start and end apart: 12, of which 6 were waited for; matrix products, arithmetic and copies ran while one was open for 22% of the time, Pallas kernels for 0%

commit v1 on v0

--- a/solution.py
+++ b/solution.py
@@ -87,7 +87,7 @@
     gap = gap[:, None]
     out = jnp.zeros(ky.shape[:-1] + (ny, ny), jnp.float32)
     for tap in range(ky.shape[-1]):
-        out = out + jnp.where(gap == tap, ky[..., tap, None, None], 0.0)
+        out = jnp.where(gap == tap, ky[..., tap, None, None], out)
     return out
 
 

time: 133 us -> 129 us (0.970)
  other arithmetic: 32.2 us -> 29 us
    add x1 -> x0, other arithmetic: 7.49 us -> none  [line_matrices(): out = out + jnp.where(gap == tap, ky[..., tap, None, None], 0.0)]
    select_n x0 -> x1, other arithmetic: none -> 4.88 us  [line_matrices(): out = jnp.where(gap == tap, ky[..., tap, None, None], out)]
  transfers between devices with their start and end apart: 12 -> 12, of which waited for: 6 -> 6; matrix products, arithmetic and copies ran while one was open for 22% -> 20% of each run, Pallas kernels for 0% -> 0%
where the time goes in v1:
time: 129 us
  starting transfers between devices  40.3 us (31%)
  waiting for transfers between devices  31.8 us (25%)
  other arithmetic  29 us (22%)
  matrix products  19.6 us (15%)
  local copies, waits for them, and re-layouts  7.1 us (6%)
    ppermute x6, waiting for transfers between devices, extended(): lax.ppermute(tail, axis, [(i, (i + 1) % count) for i in range(ends)])  27.8 us
    ppermute x6, starting transfers between devices, extended(): lax.ppermute(head, axis, [((i + 1) % count, i) for i in range(ends)])  24.5 us
    ppermute x6, starting transfers between devices, extended(): lax.ppermute(tail, axis, [(i, (i + 1) % count) for i in range(ends)])  15.8 us
    add x7, other arithmetic, tv_pass(): return field + TAU * total  7.24 us
    div x24, other arithmetic, flux(): return diff / jnp.sqrt(diff * diff + EPS_TV)  6.49 us
    dot_general x4, matrix products, plane_matrices(): jnp.einsum('qa,...ab,bp->...qp', pick_qz, wz, pick_pz, precision=HIGH)  5.23 us
    dot_general x1, matrix products, local(): jnp.einsum('vrqi,vrji->qj', spread, lines, precision=HIGH) / RANK  5.02 us
    select_n x1, other arithmetic, line_matrices(): out = jnp.where(gap == tap, ky[..., tap, None, None], out)  4.88 us
  transfers between devices with their start and end apart: 12, of which 6 were waited for; matrix products, arithmetic and copies ran while one was open for 20% of the time, Pallas kernels for 0%

profile of v1, /device:TPU:132, one launch (start us, length us, event | category | flops | bytes accessed | tf_op | source)
XLA Modules:
  0.0 128.9 jit_solution(3455226337540876487)
XLA Ops:
  0.0 4.3 %collective-permute-start.1 = (f32[8,16,512]{2,1,0:T(8,128)}, f32[8,16,512]{2,1,0:T(8,128)S(1)}, u32[]{:S(2)}, u32[]{:S(2)}) collective-permute-start(f32[8,16,512]{2,1,0:T(8,128)} %param.5), channel_id=1, source_target_pairs={{16,0},{32,16},{48,32},{64,48},{80,64},{96,80},{112,96},{128,112},... | collective-permute-start | bytes 786440 | tf_op jit(solution)/shard_map/ppermute | solution.py:29
  4.3 1.9 %collective-permute-start = (f32[8,16,512]{2,1,0:T(8,128)}, f32[8,16,512]{2,1,0:T(8,128)S(1)}, u32[]{:S(2)}, u32[]{:S(2)}) collective-permute-start(f32[8,16,512]{2,1,0:T(8,128)} %param.5), channel_id=1, source_target_pairs={{0,16},{16,32},{32,48},{48,64},{64,80},{80,96},{96,112},{112,128},... | collective-permute-start | bytes 786440 | tf_op jit(solution)/shard_map/ppermute | solution.py:27
  6.8 0.7 fusion.306
  7.7 0.7 fusion.308
  8.4 0.7 fusion.307
  9.0 0.6 fusion.305
  9.9 0.8 reduce_sum.9
  10.7 0.8 broadcast_divide_fusion
  12.7 2.3 %fusion.285 = f32[384,3,3,128]{3,0,2,1:T(8,128)} fusion(f32[384,3,3,8]{0,3,2,1:T(8,128)S(1)} %fusion.143, s32[128]{0:T(128)S(1)} %and_select_fusion.1), kind=kOutput, calls=%fused_computation.424 | convolution fusion | flops 21234688 | bytes 1880576 | tf_op jit(solution)/shard_map/qa,...ab,bp->...qp/dot_general | solution.py:78
  15.4 1.1 fusion.266
  16.8 2.3 %fusion.287 = f32[384,3,3,128]{3,0,2,1:T(8,128)} fusion(f32[384,3,3,8]{0,3,2,1:T(8,128)S(1)} %fusion.172, s32[128]{0:T(128)S(1)} %and_select_fusion.1), kind=kOutput, calls=%fused_computation.425 | convolution fusion | flops 21234688 | bytes 1880576 | tf_op jit(solution)/shard_map/qa,...ab,bp->...qp/dot_general | solution.py:78
  19.2 0.8 fusion.300
  20.0 4.0 %collective-permute-start.2 = (f32[24,8,512]{2,1,0:T(8,128)}, f32[24,8,512]{2,1,0:T(8,128)S(1)}, u32[]{:S(2)}, u32[]{:S(2)}) collective-permute-start(f32[24,8,512]{2,1,0:T(8,128)} %get-tuple-element.54), channel_id=1, source_target_pairs={{0,1},{1,2},{2,3},{3,4},{4,5},{5,6},{6,7},{7,8},{8,9},{9,10},{10,1... | collective-permute-start | bytes 1179656 | tf_op jit(solution)/shard_map/ppermute | solution.py:27
  25.1 0.9 compare_reduce_fusion
  26.3 4.1 %collective-permute-start.3 = (f32[24,8,512]{2,1,0:T(8,128)S(1)}, f32[24,8,512]{2,1,0:T(8,128)S(1)}, u32[]{:S(2)}, u32[]{:S(2)}) collective-permute-start(f32[24,8,512]{2,1,0:T(8,128)S(1)} %get-tuple-element.53), channel_id=1, source_target_pairs={{1,0},{2,1},{3,2},{4,3},{5,4},{6,5},{7,6},{8,7},{9,8},{10,9},{11,1... | collective-permute-start | bytes 1179656 | tf_op jit(solution)/shard_map/ppermute | solution.py:29
  30.4 0.7 compare_select_fusion
  31.1 8.5 %collective-permute-done.2 = f32[24,8,512]{2,1,0:T(8,128)S(1)} collective-permute-done((f32[24,8,512]{2,1,0:T(8,128)}, f32[24,8,512]{2,1,0:T(8,128)S(1)}, u32[]{:S(2)}, u32[]{:S(2)}) %collective-permute-start.2) | collective-permute-done | bytes 393248 | tf_op jit(solution)/shard_map/ppermute | solution.py:27
  39.8 3.2 %collective-permute-done.3 = f32[24,8,512]{2,1,0:T(8,128)S(1)} collective-permute-done((f32[24,8,512]{2,1,0:T(8,128)S(1)}, f32[24,8,512]{2,1,0:T(8,128)S(1)}, u32[]{:S(2)}, u32[]{:S(2)}) %collective-permute-start.3) | collective-permute-done | bytes 393248 | tf_op jit(solution)/shard_map/ppermute | solution.py:29
  43.7 0.6 rsqrt_multiply_fusion.1
  44.4 1.6 %fusion.20 = f32[22,30,512]{2,1,0:T(8,128)S(1)} fusion(f32[22,31,512]{2,1,0:T(8,128)S(1)} %rsqrt_multiply_fusion.2, f32[23,30,512]{2,1,0:T(8,128)S(1)} %rsqrt_multiply_fusion, f32[24,32,512]{2,1,0:T(8,128)S(1)} %constant_dynamic-update-slice_fusion, f32[22,30,511]{2,1,0:T(8,128)S(1)} %rsqrt_multiply_fusion.1, f32[30]{0:T(128)S(1)} %get-tuple-element.113, ...), kind=kLoop, calls=%fused_computation.27 | loop fusion | flops 5406720 | bytes 9460560 | tf_op jit(solution)/shard_map/add | solution.py:57
  46.6 0.6 rsqrt_multiply_fusion.4
  47.2 1.5 %fusion.29 = f32[20,28,512]{2,1,0:T(8,128)S(1)} fusion(f32[20,29,512]{2,1,0:T(8,128)S(1)} %rsqrt_multiply_fusion.5, f32[21,28,512]{2,1,0:T(8,128)S(1)} %rsqrt_multiply_fusion.3, f32[22,30,512]{2,1,0:T(8,128)S(1)} %fusion.20, f32[20,28,511]{2,1,0:T(8,128)S(1)} %rsqrt_multiply_fusion.4, f32[28]{0:T(128)S(1)} %get-tuple-element.109, ...), kind=kLoop, calls=%fused_computation.46 | loop fusion | flops 4587520 | bytes 8027328 | tf_op jit(solution)/shard_map/add | solution.py:57
  49.3 0.5 rsqrt_multiply_fusion.7
  49.8 1.3 %fusion.47 = f32[18,26,512]{2,1,0:T(8,128)S(1)} fusion(f32[18,27,512]{2,1,0:T(8,128)S(1)} %rsqrt_multiply_fusion.8, f32[19,26,512]{2,1,0:T(8,128)S(1)} %rsqrt_multiply_fusion.6, f32[20,28,512]{2,1,0:T(8,128)S(1)} %fusion.29, f32[18,26,511]{2,1,0:T(8,128)S(1)} %rsqrt_multiply_fusion.7, f32[26]{0:T(128)S(1)} %get-tuple-element.105, ...), kind=kLoop, calls=%fused_computation.68 | loop fusion | flops 3833856 | bytes 6708752 | tf_op jit(solution)/shard_map/add | solution.py:57
  51.9 0.8 fusion.57
  53.5 0.7 fusion.66
  54.8 0.8 fusion.75
  57.9 4.3 %collective-permute-start.5 = (bf16[4,16,512]{2,1,0:T(8,128)(2,1)S(1)}, bf16[4,16,512]{2,1,0:T(8,128)(2,1)S(1)}, u32[]{:S(2)}, u32[]{:S(2)}) collective-permute-start(bf16[4,16,512]{2,1,0:T(8,128)(2,1)S(1)} %get-tuple-element.60), channel_id=1, source_target_pairs={{16,0},{32,16},{48,32},{64,48},{80,64},{96,80},{112,96},{128,112},... | collective-permute-start | bytes 196616 | tf_op jit(solution)/shard_map/ppermute | solution.py:29
  62.1 1.9 %collective-permute-start.4 = (bf16[4,16,512]{2,1,0:T(8,128)(2,1)S(1)}, bf16[4,16,512]{2,1,0:T(8,128)(2,1)S(1)}, u32[]{:S(2)}, u32[]{:S(2)}) collective-permute-start(bf16[4,16,512]{2,1,0:T(8,128)(2,1)S(1)} %get-tuple-element.59), channel_id=1, source_target_pairs={{0,16},{16,32},{32,48},{48,64},{64,80},{80,96},{96,112},{112,128},... | collective-permute-start | bytes 196616 | tf_op jit(solution)/shard_map/ppermute | solution.py:27
  64.1 4.5 %fusion.10 = (pred[3,512,512]{2,1,0:T(8,128)(4,1)S(1)}, pred[3,512,512]{2,1,0:T(8,128)(4,1)S(1)}, pred[3,512,512]{2,1,0:T(8,128)(4,1)S(1)}, pred[3,512,512]{2,1,...) fusion(s32[3,512]{1,0:T(4,128)S(1)} %compare_select_fusion), kind=kLoop, calls=%fused_computation.12 | loop fusion | flops 8650752 | bytes 7084032 | tf_op jit(solution)/shard_map/eq | solution.py:90
  68.6 2.8 %collective-permute-done.4 = bf16[4,16,512]{2,1,0:T(8,128)(2,1)S(1)} collective-permute-done((bf16[4,16,512]{2,1,0:T(8,128)(2,1)S(1)}, bf16[4,16,512]{2,1,0:T(8,128)(2,1)S(1)}, u32[]{:S(2)}, u32[]{:S(2)}) %collective-permute-start.4) | collective-permute-done | bytes 65568 | tf_op jit(solution)/shard_map/ppermute | solution.py:27
  71.4 2.0 %collective-permute-start.7 = (bf16[16,4,512]{2,1,0:T(4,128)(2,1)S(1)}, bf16[16,4,512]{2,1,0:T(4,128)(2,1)S(1)}, u32[]{:S(2)}, u32[]{:S(2)}) collective-permute-start(bf16[16,4,512]{2,1,0:T(4,128)(2,1)S(1)} %get-tuple-element.58), channel_id=1, source_target_pairs={{1,0},{2,1},{3,2},{4,3},{5,4},{6,5},{7,6},{8,7},{9,8},{10,9},{11,1... | collective-permute-start | bytes 196616 | tf_op jit(solution)/shard_map/ppermute | solution.py:29
  73.4 3.9 %collective-permute-start.6 = (bf16[16,4,512]{2,1,0:T(4,128)(2,1)S(1)}, bf16[16,4,512]{2,1,0:T(4,128)(2,1)S(1)}, u32[]{:S(2)}, u32[]{:S(2)}) collective-permute-start(bf16[16,4,512]{2,1,0:T(4,128)(2,1)S(1)} %get-tuple-element.57), channel_id=1, source_target_pairs={{0,1},{1,2},{2,3},{3,4},{4,5},{5,6},{6,7},{7,8},{8,9},{9,10},{10,1... | collective-permute-start | bytes 196616 | tf_op jit(solution)/shard_map/ppermute | solution.py:27
  77.3 4.9 %select_select_fusion = f32[3,3,512,512]{3,2,0,1:T(8,128)S(1)} fusion(f32[3,3]{0,1:T(4,128)S(1)} %bitcast.90, f32[3,3]{0,1:T(4,128)S(1)} %bitcast.91, f32[3,3]{0,1:T(4,128)S(1)} %bitcast.92, f32[3,3]{0,1:T(4,128)S(1)} %bitcast.93, f32[3,3]{0,1:T(4,128)S(1)} %bitcast.94, f32[3,3]{0,1:T(4,128)S(1)} %bitcast.95, f32[3,3]{0,1:T(4,128)S(1)} %bitcast.96, ...), kind=kLoop, calls=%fused_computation.2 | loop fusion | flops 21233664 | bytes 16515396 | tf_op jit(solution)/shard_map/jit(_where)/select_n | solution.py:90
  82.4 1.5 %fusion.11 = f32[3,3,128,512]{3,2,1,0:T(8,128)S(1)} fusion(bf16[384,512,1,1]{1,0,3,2:T(8,128)(2,1)S(1)} %bitcast.85, f32[384,3,3,128]{3,0,2,1:T(8,128)S(1)} %copy-done, f32[384,3,3,128]{3,0,2,1:T(8,128)S(1)} %fusion.266), kind=kOutput, calls=%fused_computation.13 | convolution fusion | flops 1359396864 | bytes 6291456 | tf_op jit(solution)/shard_map/vrqp,pj->vrqj/dot_general | solution.py:135
  83.9 3.6 %fusion.40 = f32[3,128,512]{2,1,0:T(8,128)S(1)} fusion(f32[3,3,128,512]{3,2,1,0:T(8,128)S(1)} %fusion.11, f32[3,3,512,512]{3,2,0,1:T(8,128)S(1)} %select_select_fusion), kind=kOutput, calls=%fused_computation.59 | convolution fusion | flops 1812332544 | bytes 12582912 | tf_op jit(solution)/shard_map/vrqi,vrij->vqj/dot_general | solution.py:136
  87.8 4.1 %collective-permute-start.9 = (bf16[3,4,16,512]{3,2,1,0:T(8,128)(2,1)S(1)}, bf16[3,4,16,512]{3,2,1,0:T(8,128)(2,1)S(1)}, u32[]{:S(2)}, u32[]{:S(2)}) collective-permute-start(bf16[3,4,16,512]{3,2,1,0:T(8,128)(2,1)S(1)} %get-tuple-element.56), channel_id=1, source_target_pairs={{16,0},{32,16},{48,32},{64,48},{80,64},{96,80},{112,96},{128,112},... | collective-permute-start | bytes 589832 | tf_op jit(solution)/shard_map/ppermute | solution.py:29
  91.9 1.9 %collective-permute-start.8 = (bf16[3,4,16,512]{3,2,1,0:T(8,128)(2,1)S(1)}, bf16[3,4,16,512]{3,2,1,0:T(8,128)(2,1)S(1)}, u32[]{:S(2)}, u32[]{:S(2)}) collective-permute-start(bf16[3,4,16,512]{3,2,1,0:T(8,128)(2,1)S(1)} %get-tuple-element.55), channel_id=1, source_target_pairs={{0,16},{16,32},{32,48},{48,64},{64,80},{80,96},{96,112},{112,128},... | collective-permute-start | bytes 589832 | tf_op jit(solution)/shard_map/ppermute | solution.py:27
  94.3 0.8 collective-permute-done.9
  95.1 10.1 %collective-permute-done.8 = bf16[3,4,16,512]{3,2,1,0:T(8,128)(2,1)S(1)} collective-permute-done((bf16[3,4,16,512]{3,2,1,0:T(8,128)(2,1)S(1)}, bf16[3,4,16,512]{3,2,1,0:T(8,128)(2,1)S(1)}, u32[]{:S(2)}, u32[]{:S(2)}) %collective-permute-start.8) | collective-permute-done | bytes 196640 | tf_op jit(solution)/shard_map/ppermute | solution.py:27
  105.4 5.7 %collective-permute-start.11 = (bf16[3,16,4,512]{3,2,1,0:T(4,128)(2,1)S(1)}, bf16[3,16,4,512]{3,2,1,0:T(4,128)(2,1)S(1)}, u32[]{:S(2)}, u32[]{:S(2)}) collective-permute-start(bf16[3,16,4,512]{3,2,1,0:T(4,128)(2,1)S(1)} %get-tuple-element.52), channel_id=1, source_target_pairs={{1,0},{2,1},{3,2},{4,3},{5,4},{6,5},{7,6},{8,7},{9,8},{10,9},{11,1... | collective-permute-start | bytes 589832 | tf_op jit(solution)/shard_map/ppermute | solution.py:29
  111.1 2.2 %collective-permute-start.10 = (bf16[3,16,4,512]{3,2,1,0:T(4,128)(2,1)S(1)}, bf16[3,16,4,512]{3,2,1,0:T(4,128)(2,1)S(1)}, u32[]{:S(2)}, u32[]{:S(2)}) collective-permute-start(bf16[3,16,4,512]{3,2,1,0:T(4,128)(2,1)S(1)} %get-tuple-element.51), channel_id=1, source_target_pairs={{0,1},{1,2},{2,3},{3,4},{4,5},{5,6},{6,7},{7,8},{8,9},{9,10},{10,1... | collective-permute-start | bytes 589832 | tf_op jit(solution)/shard_map/ppermute | solution.py:27
  113.4 1.1 multiply_bitcast_fusion
  114.5 6.3 %collective-permute-done.10 = bf16[3,16,4,512]{3,2,1,0:T(4,128)(2,1)S(1)} collective-permute-done((bf16[3,16,4,512]{3,2,1,0:T(4,128)(2,1)S(1)}, bf16[3,16,4,512]{3,2,1,0:T(4,128)(2,1)S(1)}, u32[]{:S(2)}, u32[]{:S(2)}) %collective-permute-start.10) | collective-permute-done | bytes 196640 | tf_op jit(solution)/shard_map/ppermute | solution.py:27
  120.8 0.8 pad_maximum_fusion
  121.7 1.5 %fusion.13 = f32[3,3,128,512]{3,2,0,1:T(8,128)S(1)} fusion(bf16[3,384,512,1]{2,1,0,3:T(8,128)(2,1)S(1)} %bitcast.83, f32[3,3,128,384]{2,3,1,0:T(8,128)S(1)} %multiply_bitcast_fusion), kind=kOutput, calls=%fused_computation.15 | convolution fusion | flops 1358954496 | bytes 5308416 | tf_op jit(solution)/shard_map/vrqp,vpj->vrqj/dot_general | solution.py:146
  123.1 5.0 %fusion.52 = f32[128,512]{1,0:T(8,128)S(1)} fusion(f32[3,3,128,512]{3,2,0,1:T(8,128)S(1)} %fusion.13, f32[3,3,512,512]{3,2,0,1:T(8,128)S(1)} %select_select_fusion), kind=kOutput, calls=%fused_computation.81 | convolution fusion | flops 1812004864 | bytes 12058624 | tf_op jit(solution)/shard_map/vrqi,vrji->qj/dot_general | solution.py:147
  128.1 0.7 multiply_multiply_fusion
  (152 shorter events, 11.3 us)
Async XLA Ops:
  0.0 19.2 %collective-permute-start.1 = (f32[8,16,512]{2,1,0:T(8,128)}, f32[8,16,512]{2,1,0:T(8,128)S(1)}, u32[]{:S(2)}, u32[]{:S(2)}) collective-permute-start(f32[8,16,512]{2,1,0:T(8,128)} %param.5), channel_id=1, source_target_pairs={{16,0},{32,16},{48,32},{64,48},{80,64},{96,80},{112,96},{128,112},... | collective-permute-start | bytes 786440 | tf_op jit(solution)/shard_map/ppermute | solution.py:29
  4.3 14.9 %collective-permute-start = (f32[8,16,512]{2,1,0:T(8,128)}, f32[8,16,512]{2,1,0:T(8,128)S(1)}, u32[]{:S(2)}, u32[]{:S(2)}) collective-permute-start(f32[8,16,512]{2,1,0:T(8,128)} %param.5), channel_id=1, source_target_pairs={{0,16},{16,32},{32,48},{48,64},{64,80},{80,96},{96,112},{112,128},... | collective-permute-start | bytes 786440 | tf_op jit(solution)/shard_map/ppermute | solution.py:27
  9.8 5.6 %copy-start.4 = (pred[16,24]{1,0:T(8,128)(4,1)}, pred[16,24]{1,0:T(8,128)(4,1)S(1)}, u32[]{:S(2)}) copy-start(pred[16,24]{1,0:T(8,128)(4,1)S(1)} %get-tuple-element.130) | copy-start | bytes 1156
  9.8 5.6 %copy-start.6 = (pred[16,24]{1,0:T(8,128)(4,1)}, pred[16,24]{1,0:T(8,128)(4,1)S(1)}, u32[]{:S(2)}) copy-start(pred[16,24]{1,0:T(8,128)(4,1)S(1)} %get-tuple-element.131) | copy-start | bytes 1156
  9.8 5.5 %copy-start.8 = (pred[16,24]{1,0:T(8,128)(4,1)}, pred[16,24]{1,0:T(8,128)(4,1)S(1)}, u32[]{:S(2)}) copy-start(pred[16,24]{1,0:T(8,128)(4,1)S(1)} %get-tuple-element.132) | copy-start | bytes 1156
  9.8 5.5 %copy-start.10 = (pred[16,24]{1,0:T(8,128)(4,1)}, pred[16,24]{1,0:T(8,128)(4,1)S(1)}, u32[]{:S(2)}) copy-start(pred[16,24]{1,0:T(8,128)(4,1)S(1)} %get-tuple-element.133) | copy-start | bytes 1156
  9.8 5.5 %copy-start.12 = (pred[16,24]{1,0:T(8,128)(4,1)}, pred[16,24]{1,0:T(8,128)(4,1)S(1)}, u32[]{:S(2)}) copy-start(pred[16,24]{1,0:T(8,128)(4,1)S(1)} %get-tuple-element.134) | copy-start | bytes 1156
  9.8 5.5 %copy-start.14 = (pred[16,24]{1,0:T(8,128)(4,1)}, pred[16,24]{1,0:T(8,128)(4,1)S(1)}, u32[]{:S(2)}) copy-start(pred[16,24]{1,0:T(8,128)(4,1)S(1)} %get-tuple-element.135) | copy-start | bytes 1156
  9.9 5.5 %copy-start.16 = (pred[16,24]{1,0:T(8,128)(4,1)}, pred[16,24]{1,0:T(8,128)(4,1)S(1)}, u32[]{:S(2)}) copy-start(pred[16,24]{1,0:T(8,128)(4,1)S(1)} %fusion.264) | copy-start | bytes 1156
  9.9 5.5 %copy-start.18 = (s32[384]{0:T(512)}, s32[384]{0:T(512)S(1)}, u32[]{:S(2)}) copy-start(s32[384]{0:T(512)S(1)} %fusion.280) | copy-start | bytes 4612
  9.9 5.5 %copy-start.28 = (s32[128]{0:T(128)}, s32[128]{0:T(128)S(1)}, u32[]{:S(2)}) copy-start(s32[128]{0:T(128)S(1)} %and_select_fusion) | copy-start | bytes 1540
  16.5 2.6 %copy-start.3 = (f32[8,16,512]{2,1,0:T(8,128)S(1)}, f32[8,16,512]{2,1,0:T(8,128)}, u32[]{:S(2)}) copy-start(f32[8,16,512]{2,1,0:T(8,128)} %param.5) | copy-start | bytes 786436
  20.0 19.7 %collective-permute-start.2 = (f32[24,8,512]{2,1,0:T(8,128)}, f32[24,8,512]{2,1,0:T(8,128)S(1)}, u32[]{:S(2)}, u32[]{:S(2)}) collective-permute-start(f32[24,8,512]{2,1,0:T(8,128)} %get-tuple-element.54), channel_id=1, source_target_pairs={{0,1},{1,2},{2,3},{3,4},{4,5},{5,6},{6,7},{7,8},{8,9},{9,10},{10,1... | collective-permute-start | bytes 1179656 | tf_op jit(solution)/shard_map/ppermute | solution.py:27
  26.3 16.7 %collective-permute-start.3 = (f32[24,8,512]{2,1,0:T(8,128)S(1)}, f32[24,8,512]{2,1,0:T(8,128)S(1)}, u32[]{:S(2)}, u32[]{:S(2)}) collective-permute-start(f32[24,8,512]{2,1,0:T(8,128)S(1)} %get-tuple-element.53), channel_id=1, source_target_pairs={{1,0},{2,1},{3,2},{4,3},{5,4},{6,5},{7,6},{8,7},{9,8},{10,9},{11,1... | collective-permute-start | bytes 1179656 | tf_op jit(solution)/shard_map/ppermute | solution.py:29
  55.7 0.6 copy-start.22
  55.7 0.7 copy-start.23
  55.7 0.7 copy-start.24
  55.7 0.7 copy-start.25
  56.9 0.6 copy-start.20
  56.9 0.6 copy-start.21
  56.9 0.7 copy-start.26
  56.9 0.7 copy-start.27
  57.9 10.7 %collective-permute-start.5 = (bf16[4,16,512]{2,1,0:T(8,128)(2,1)S(1)}, bf16[4,16,512]{2,1,0:T(8,128)(2,1)S(1)}, u32[]{:S(2)}, u32[]{:S(2)}) collective-permute-start(bf16[4,16,512]{2,1,0:T(8,128)(2,1)S(1)} %get-tuple-element.60), channel_id=1, source_target_pairs={{16,0},{32,16},{48,32},{64,48},{80,64},{96,80},{112,96},{128,112},... | collective-permute-start | bytes 196616 | tf_op jit(solution)/shard_map/ppermute | solution.py:29
  62.1 9.2 %collective-permute-start.4 = (bf16[4,16,512]{2,1,0:T(8,128)(2,1)S(1)}, bf16[4,16,512]{2,1,0:T(8,128)(2,1)S(1)}, u32[]{:S(2)}, u32[]{:S(2)}) collective-permute-start(bf16[4,16,512]{2,1,0:T(8,128)(2,1)S(1)} %get-tuple-element.59), channel_id=1, source_target_pairs={{0,16},{16,32},{32,48},{48,64},{64,80},{80,96},{96,112},{112,128},... | collective-permute-start | bytes 196616 | tf_op jit(solution)/shard_map/ppermute | solution.py:27
  71.4 10.8 %collective-permute-start.7 = (bf16[16,4,512]{2,1,0:T(4,128)(2,1)S(1)}, bf16[16,4,512]{2,1,0:T(4,128)(2,1)S(1)}, u32[]{:S(2)}, u32[]{:S(2)}) collective-permute-start(bf16[16,4,512]{2,1,0:T(4,128)(2,1)S(1)} %get-tuple-element.58), channel_id=1, source_target_pairs={{1,0},{2,1},{3,2},{4,3},{5,4},{6,5},{7,6},{8,7},{9,8},{10,9},{11,1... | collective-permute-start | bytes 196616 | tf_op jit(solution)/shard_map/ppermute | solution.py:29
  73.4 8.8 %collective-permute-start.6 = (bf16[16,4,512]{2,1,0:T(4,128)(2,1)S(1)}, bf16[16,4,512]{2,1,0:T(4,128)(2,1)S(1)}, u32[]{:S(2)}, u32[]{:S(2)}) collective-permute-start(bf16[16,4,512]{2,1,0:T(4,128)(2,1)S(1)} %get-tuple-element.57), channel_id=1, source_target_pairs={{0,1},{1,2},{2,3},{3,4},{4,5},{5,6},{6,7},{7,8},{8,9},{9,10},{10,1... | collective-permute-start | bytes 196616 | tf_op jit(solution)/shard_map/ppermute | solution.py:27
  77.3 5.1 %copy-start = (f32[384,3,3,128]{3,0,2,1:T(8,128)S(1)}, f32[384,3,3,128]{3,0,2,1:T(8,128)}, u32[]{:S(2)}) copy-start(f32[384,3,3,128]{3,0,2,1:T(8,128)} %fusion.285) | copy-start | bytes 5308420
  83.9 3.7 %copy-start.2 = (bf16[3,8,16,512]{3,2,1,0:T(8,128)(2,1)S(1)}, bf16[3,8,16,512]{3,2,1,0:T(8,128)(2,1)}, u32[]{:S(2)}) copy-start(bf16[3,8,16,512]{3,2,1,0:T(8,128)(2,1)} %param.6) | copy-start | bytes 1179652
  87.5 6.4 %copy-start.5 = (pred[16,24]{1,0:T(8,128)(4,1)S(1)}, pred[16,24]{1,0:T(8,128)(4,1)}, u32[]{:S(2)}) copy-start(pred[16,24]{1,0:T(8,128)(4,1)} %copy-done.4) | copy-start | bytes 1156
  87.5 6.4 %copy-start.7 = (pred[16,24]{1,0:T(8,128)(4,1)S(1)}, pred[16,24]{1,0:T(8,128)(4,1)}, u32[]{:S(2)}) copy-start(pred[16,24]{1,0:T(8,128)(4,1)} %copy-done.6) | copy-start | bytes 1156
  87.5 6.4 %copy-start.9 = (pred[16,24]{1,0:T(8,128)(4,1)S(1)}, pred[16,24]{1,0:T(8,128)(4,1)}, u32[]{:S(2)}) copy-start(pred[16,24]{1,0:T(8,128)(4,1)} %copy-done.8) | copy-start | bytes 1156
  87.5 6.4 %copy-start.11 = (pred[16,24]{1,0:T(8,128)(4,1)S(1)}, pred[16,24]{1,0:T(8,128)(4,1)}, u32[]{:S(2)}) copy-start(pred[16,24]{1,0:T(8,128)(4,1)} %copy-done.10) | copy-start | bytes 1156
  87.5 6.4 %copy-start.13 = (pred[16,24]{1,0:T(8,128)(4,1)S(1)}, pred[16,24]{1,0:T(8,128)(4,1)}, u32[]{:S(2)}) copy-start(pred[16,24]{1,0:T(8,128)(4,1)} %copy-done.12) | copy-start | bytes 1156
  87.6 6.4 %copy-start.15 = (pred[16,24]{1,0:T(8,128)(4,1)S(1)}, pred[16,24]{1,0:T(8,128)(4,1)}, u32[]{:S(2)}) copy-start(pred[16,24]{1,0:T(8,128)(4,1)} %copy-done.14) | copy-start | bytes 1156
  87.6 6.4 %copy-start.17 = (pred[16,24]{1,0:T(8,128)(4,1)S(1)}, pred[16,24]{1,0:T(8,128)(4,1)}, u32[]{:S(2)}) copy-start(pred[16,24]{1,0:T(8,128)(4,1)} %copy-done.16) | copy-start | bytes 1156
  87.6 6.4 %copy-start.19 = (s32[384]{0:T(512)S(1)}, s32[384]{0:T(512)}, u32[]{:S(2)}) copy-start(s32[384]{0:T(512)} %copy-done.18) | copy-start | bytes 4612
  87.8 25.5 %copy-start.1 = (f32[384,3,3,128]{3,0,2,1:T(8,128)S(1)}, f32[384,3,3,128]{3,0,2,1:T(8,128)}, u32[]{:S(2)}) copy-start(f32[384,3,3,128]{3,0,2,1:T(8,128)} %fusion.287) | copy-start | bytes 5308420
  87.8 25.5 %copy-start.29 = (s32[128]{0:T(128)S(1)}, s32[128]{0:T(128)}, u32[]{:S(2)}) copy-start(s32[128]{0:T(128)} %copy-done.28) | copy-start | bytes 1540
  87.8 7.3 %collective-permute-start.9 = (bf16[3,4,16,512]{3,2,1,0:T(8,128)(2,1)S(1)}, bf16[3,4,16,512]{3,2,1,0:T(8,128)(2,1)S(1)}, u32[]{:S(2)}, u32[]{:S(2)}) collective-permute-start(bf16[3,4,16,512]{3,2,1,0:T(8,128)(2,1)S(1)} %get-tuple-element.56), channel_id=1, source_target_pairs={{16,0},{32,16},{48,32},{64,48},{80,64},{96,80},{112,96},{128,112},... | collective-permute-start | bytes 589832 | tf_op jit(solution)/shard_map/ppermute | solution.py:29
  91.9 13.3 %collective-permute-start.8 = (bf16[3,4,16,512]{3,2,1,0:T(8,128)(2,1)S(1)}, bf16[3,4,16,512]{3,2,1,0:T(8,128)(2,1)S(1)}, u32[]{:S(2)}, u32[]{:S(2)}) collective-permute-start(bf16[3,4,16,512]{3,2,1,0:T(8,128)(2,1)S(1)} %get-tuple-element.55), channel_id=1, source_target_pairs={{0,16},{16,32},{32,48},{48,64},{64,80},{80,96},{96,112},{112,128},... | collective-permute-start | bytes 589832 | tf_op jit(solution)/shard_map/ppermute | solution.py:27
  105.4 9.1 %collective-permute-start.11 = (bf16[3,16,4,512]{3,2,1,0:T(4,128)(2,1)S(1)}, bf16[3,16,4,512]{3,2,1,0:T(4,128)(2,1)S(1)}, u32[]{:S(2)}, u32[]{:S(2)}) collective-permute-start(bf16[3,16,4,512]{3,2,1,0:T(4,128)(2,1)S(1)} %get-tuple-element.52), channel_id=1, source_target_pairs={{1,0},{2,1},{3,2},{4,3},{5,4},{6,5},{7,6},{8,7},{9,8},{10,9},{11,1... | collective-permute-start | bytes 589832 | tf_op jit(solution)/shard_map/ppermute | solution.py:29
  111.1 9.7 %collective-permute-start.10 = (bf16[3,16,4,512]{3,2,1,0:T(4,128)(2,1)S(1)}, bf16[3,16,4,512]{3,2,1,0:T(4,128)(2,1)S(1)}, u32[]{:S(2)}, u32[]{:S(2)}) collective-permute-start(bf16[3,16,4,512]{3,2,1,0:T(4,128)(2,1)S(1)} %get-tuple-element.51), channel_id=1, source_target_pairs={{0,1},{1,2},{2,3},{3,4},{4,5},{5,6},{6,7},{7,8},{8,9},{9,10},{10,1... | collective-permute-start | bytes 589832 | tf_op jit(solution)/shard_map/ppermute | solution.py:27
